TPU v7x, 512 devices: a whole 4x8x8 slice. The times are simulated.
512 devices in a mesh: doc: 16 (over z_lo, y), label: 32 (over x, z_hi, core).
Axes of the slice: x: 4, y: 8, z: 8 (z_hi: 4, z_lo: 2; z = z_hi * 2 + z_lo), core: 2. Of those that a mesh axis runs over, the one named last changes fastest.
Arguments:
- doc_embed: bfloat16 [16384, 768], P(('doc', 'label')), may hold values from -0.59765625 to 0.59765625
- classifier: bfloat16 [32768, 768], P('label'), may hold values from -4.28125 to 4.28125
- centroids: bfloat16 [256, 768], P('doc'), may hold values from -4.28125 to 4.28125
- shortlist: int32 [16384, 32], P(('doc', 'label')), may hold values from 0 to 255, all different within a row
- positives: int32 [16384, 4], P(('doc', 'label')), may hold values from 0 to 4095
Outputs:
- grad_classifier: bfloat16 [32768, 768], P('label')
- grad_centroids: float32 [256, 768], P('doc')
- grad_docs: bfloat16 [16384, 768], P(('doc', 'label'))
Inputs may be any that keep to these rules, and one draw needn't show every extreme that they name: `shortlist`: each row names 32 different clusters; every cluster is named by some row.
All inputs are finite; a program needn't handle non-finite values.
Results may differ from a plain program's by a relative error of at most 0.015.
Values may be sent and summed in bfloat16 or wider, within the bound.
No kernel may reach another device: no remote copies, remote signals or barrier semaphores. Data moves between devices by JAX's collectives and lax.ppermute only.
A program may use at most 64 MiB of HBM per device.

v0:
```python
import jax
import jax.numpy as jnp
from jax import lax
from jax.sharding import PartitionSpec as P

CLS = 128
LOSS_WEIGHT = 0.125


def tile_grads(rows, short_rows, pos_rows, classifier, cent_rows, cluster_base):
    labels_dev = classifier.shape[0]
    local_clusters = cluster_base + jnp.arange(labels_dev // CLS, dtype=jnp.int32)
    local_labels = cluster_base * CLS + jnp.arange(labels_dev, dtype=jnp.int32)
    logits = jnp.einsum("nd,ld->nl", rows, classifier, preferred_element_type=jnp.float32)
    member = jnp.any(short_rows[:, :, None] == local_clusters[None, None, :], axis=1)
    mask = jnp.repeat(member, CLS, axis=1)
    target = jnp.any(pos_rows[:, :, None] == local_labels[None, None, :], axis=1)
    grad = (
        LOSS_WEIGHT
        * (jax.nn.sigmoid(logits) - target.astype(jnp.float32))
        * mask.astype(jnp.float32)
    ).astype(jnp.bfloat16)
    meta_logits = jnp.einsum("nd,cd->nc", rows, cent_rows, preferred_element_type=jnp.float32)
    pos_clusters = pos_rows // CLS
    meta_target = jnp.any(pos_clusters[:, :, None] == local_clusters[None, None, :], axis=1)
    meta_grad = (
        LOSS_WEIGHT * (jax.nn.sigmoid(meta_logits) - meta_target.astype(jnp.float32))
    ).astype(jnp.bfloat16)
    return (grad, meta_grad)


def body(doc_embed, classifier, centroids, shortlist, positives):
    labels_dev = classifier.shape[0]
    cl_here = labels_dev // CLS
    per_doc = centroids.shape[0]
    label_index = lax.axis_index("label")
    cluster_base = label_index * cl_here
    pos_cluster = jnp.take_along_axis(shortlist, positives // CLS, axis=1)
    pos_label = pos_cluster * CLS + positives % CLS
    all_cent = lax.all_gather(centroids, "doc", axis=0, tiled=True)
    cent_rows = lax.dynamic_slice_in_dim(all_cent, cluster_base, cl_here, 0)
    rows, short_rows, pos_rows = (
        lax.all_gather(doc_embed, "label", axis=0, tiled=True),
        lax.all_gather(shortlist, "label", axis=0, tiled=True),
        lax.all_gather(pos_label, "label", axis=0, tiled=True),
    )
    grad, meta_grad = tile_grads(rows, short_rows, pos_rows, classifier, cent_rows, cluster_base)
    class_acc = jnp.einsum("nl,nd->ld", grad, rows, preferred_element_type=jnp.float32)
    cent_acc = jnp.einsum("nc,nd->cd", meta_grad, rows, preferred_element_type=jnp.float32)
    input_sum = lax.psum_scatter(
        (
            jnp.dot(grad, classifier, preferred_element_type=jnp.float32)
            + jnp.dot(meta_grad, cent_rows, preferred_element_type=jnp.float32)
        ).astype(jnp.bfloat16),
        "label",
        scatter_dimension=0,
        tiled=True,
    )
    grad_classifier = lax.psum(class_acc.astype(jnp.bfloat16), "doc")
    cent_summed = lax.psum(cent_acc, "doc")
    cent_whole = lax.all_gather(cent_summed, "label", axis=0, tiled=True)
    grad_centroids = lax.dynamic_slice_in_dim(
        cent_whole, lax.axis_index("doc") * per_doc, per_doc, 0
    )
    return (grad_classifier, grad_centroids, input_sum)


def solution(mesh):
    in_specs = (
        P(("doc", "label"), None),
        P("label", None),
        P("doc", None),
        P(("doc", "label"), None),
        P(("doc", "label"), None),
    )
    out_specs = (P("label", None), P("doc", None), P(("doc", "label"), None))
    return jax.shard_map(body, mesh=mesh, in_specs=in_specs, out_specs=out_specs, check_vma=False)
```

profile of v0, /device:TPU:8, one launch (start us, length us, event | category | flops | bytes accessed | tf_op | source)
XLA Modules:
  0.0 373.3 jit_solution(2617783042345759563)
XLA Ops:
  7.2 0.0 all-gather.3.cloned.1.call-start
  7.2 0.7 all-gather.3.cloned.1.call-update
  7.9 0.0 all-reduce.2.cloned.1.call-start
  8.0 0.7 bitcast_or_fusion
  8.7 0.1 copy.47
  8.8 0.1 reshape.31
  8.9 1.3 gather_fusion
  10.2 0.1 reshape.34
  10.3 0.1 copy.48
  10.4 50.2 %all-gather = s32[32,32,4]{1,2,0:T(4,128)S(1)} all-gather(s32[1,32,4]{1,2,0:T(4,128)S(1)} %fusion.12), channel_id=1, replica_groups=mesh['doc'=16,'label'=32] {'label'}, dimensions={0}, use_global_device_ids=true | all-gather | bytes 16896 | tf_op jit(solution)/shard_map/all_gather | solution.py:45
  60.6 0.1 reshape.43
  60.7 41.3 %all_gather.15 = s32[1024,32]{1,0:T(8,128)S(1)} all-gather(s32[32,32]{1,0:T(8,128)S(1)} %copy-done.1), channel_id=1, replica_groups=mesh['doc'=16,'label'=32] {'label'}, dimensions={0}, use_global_device_ids=true | all-gather | bytes 135168 | tf_op jit(solution)/shard_map/all_gather | solution.py:44
  102.1 0.2 copy.45
  102.2 0.2 compare_reduce_fusion.1
  102.5 0.3 copy.46
  102.7 3.8 %compare_reduce_fusion = pred[1024,1024]{1,0:T(8,128)(4,1)} fusion(s32[1024]{0:T(1024)S(1)} %iota_add_fusion, s32[1024,4]{0,1:T(4,128)S(1)} %reshape.43), kind=kLoop, calls=%fused_computation.1 | loop fusion | flops 7340032 | bytes 1069056 | tf_op jit(solution)/shard_map/reduce_or | solution.py:17
  106.6 3.2 broadcast_in_dim.6
  109.7 4.6 %select_convert_fusion = bf16[1024,1024]{1,0:T(8,128)(2,1)S(1)} fusion(pred[1024,1024]{1,0:T(8,128)(4,1)} %compare_reduce_fusion, pred[128,8,8,128]{3,2,1,0:T(8,128)(4,1)S(1)} %bitcast.29, bf16[1024,768]{1,0:T(8,128)(2,1)} %all-gather.3.cloned.1.call-done, bf16[1024,768]{1,0:T(8,128)(2,1)S(1)} %copy-done), kind=kOutput, calls=%fused_computation.2 | convolution fusion | flops 1619001344 | bytes 7340032 | tf_op jit(solution)/shard_map/nd,ld->nl/dot_general | solution.py:14
  114.3 1.3 copy-done.5
  115.7 3.0 convolution_convert_fusion
  118.7 0.0 reduce-scatter.2.cloned.1.call-start
  118.8 0.1 compare_reduce_fusion.2
  118.9 35.4 %all_gather.18 = bf16[256,768]{1,0:T(8,128)(2,1)S(1)} all-gather(bf16[16,768]{1,0:T(8,128)(2,1)S(1)} %copy-done.3), channel_id=1, replica_groups=mesh['doc'=16,'label'=32] {'doc'}, dimensions={0}, use_global_device_ids=true | all-gather | bytes 417792 | tf_op jit(solution)/shard_map/all_gather | solution.py:40
  154.3 0.5 fusion.6
  154.8 3.4 fusion.17
  158.2 1.8 add_convert_fusion
  160.1 0.3 fusion.16
  160.4 59.2 %psum.15 = f32[8,768]{1,0:T(8,128)S(1)} all-reduce(f32[8,768]{1,0:T(8,128)S(1)} %fusion.16), channel_id=1, replica_groups=mesh['doc'=16,'label'=32] {'doc'}, use_global_device_ids=true, to_apply=%region_4.5 | all-reduce | flops 6144 | bytes 49152 | tf_op jit(solution)/shard_map/psum | solution.py:60
  219.6 44.9 %all_gather.19 = f32[256,768]{1,0:T(8,128)S(1)} all-gather(f32[8,768]{1,0:T(8,128)S(1)} %psum.15), channel_id=1, replica_groups=mesh['doc'=16,'label'=32] {'label'}, dimensions={0}, use_global_device_ids=true | all-gather | bytes 811008 | tf_op jit(solution)/shard_map/all_gather | solution.py:61
  264.5 0.6 constant_dynamic-slice_fusion
  265.1 99.0 %reduce-scatter.2.cloned.1.call-done = bf16[32,768]{1,0:T(8,128)(2,1)} async-done(((bf16[1024,768]{1,0:T(8,128)(2,1)}), bf16[32,768]{1,0:T(8,128)(2,1)}) %reduce-scatter.2.cloned.1.call-update) | async-done | bytes 49168 | tf_op jit(solution)/shard_map/reduce_scatter | solution.py:50
  364.1 2.7 copy.53
  (20 shorter events, 0.1 us)
Async XLA Ops:
  7.2 102.6 %copy-start = (bf16[1024,768]{1,0:T(8,128)(2,1)S(1)}, bf16[1024,768]{1,0:T(8,128)(2,1)}, u32[]{:S(2)}) copy-start(bf16[1024,768]{1,0:T(8,128)(2,1)} %param.6) | copy-start | bytes 4718596
  7.2 1.7 copy-start.1
  7.2 99.4 %all-gather.3.cloned.1.call-start = ((), (), s32[]{:S(2)}) async-start(), calls=%async_computation.1 | async-start | bytes 1622016 | tf_op jit(solution)/shard_map/all_gather | solution.py:43
  7.9 257.2 %all-reduce.2.cloned.1.call-start = ((), (), s32[]{:S(2)}) async-start(), calls=%async_computation.2 | async-start | bytes 3145728 | tf_op jit(solution)/shard_map/psum | solution.py:59
  8.9 1.5 copy-start.4
  109.7 5.9 %copy-start.2 = (bf16[1024,768]{1,0:T(8,128)(2,1)S(1)}, bf16[1024,768]{1,0:T(8,128)(2,1)}, u32[]{:S(2)}) copy-start(bf16[1024,768]{1,0:T(8,128)(2,1)} %all-gather.3.cloned.1.call-done) | copy-start | bytes 4718596
  114.3 1.4 copy-start.5
  115.7 3.2 copy-start.3
  118.7 245.4 %reduce-scatter.2.cloned.1.call-start = ((), (), s32[]{:S(2)}) async-start(), calls=%async_computation.3 | async-start | bytes 1622016 | tf_op jit(solution)/shard_map/reduce_scatter | solution.py:50
Sparse Core Ops, SparseCore 0:
  11.1 64.0 all-gather.2
  118.9 141.9 all-reduce.1
  265.9 98.2 reduce-scatter.1
where the time goes:
time: 374 us; the launch traced here: 373 us
  blocking collectives  231 us (62%)
  waiting for transfers between devices  99.7 us (27%)
  between operations  13.9 us (4%)
  matrix products  13.6 us (4%)
  local copies, waits for them, and re-layouts  9.97 us (3%)
  other arithmetic  4.87 us (1%)
    reduce_scatter x1, waiting for transfers between devices, body(): lax.psum_scatter((jnp.dot(grad, classifier, preferred_element_type=jnp.fl...  99 us
    psum x1, blocking collectives, body(): cent_summed = lax.psum(cent_acc, 'doc')  59.2 us
    all_gather x1, blocking collectives, body(): lax.all_gather(pos_label, 'label', axis=0, tiled=True)  50.2 us
    all_gather x1, blocking collectives, body(): cent_whole = lax.all_gather(cent_summed, 'label', axis=0, tiled=True)  44.9 us
    all_gather x1, blocking collectives, body(): lax.all_gather(shortlist, 'label', axis=0, tiled=True)  41.3 us
    all_gather x1, blocking collectives, body(): all_cent = lax.all_gather(centroids, 'doc', axis=0, tiled=True)  35.4 us
  transfers between devices with their start and end apart: 3, of which 1 were waited for; matrix products, arithmetic and copies ran while one was open for 4% of the time, Pallas kernels for 0%

commit v1 on v0

--- a/solution.py
+++ b/solution.py
@@ -42,7 +42,9 @@
     rows, short_rows, pos_rows = (
         lax.all_gather(doc_embed, "label", axis=0, tiled=True),
         lax.all_gather(shortlist, "label", axis=0, tiled=True),
-        lax.all_gather(pos_label, "label", axis=0, tiled=True),
+        jnp.concatenate(
+            lax.all_to_all(jnp.stack([pos_label] * lax.axis_size("label")), "label", 0, 0), axis=0
+        ),
     )
     grad, meta_grad = tile_grads(rows, short_rows, pos_rows, classifier, cent_rows, cluster_base)
     class_acc = jnp.einsum("nl,nd->ld", grad, rows, preferred_element_type=jnp.float32)

time: 374 us -> 342 us (0.914)
  blocking collectives: 231 us -> 183 us
  starting transfers between devices: 0.12 us -> 13.3 us
    all_gather x1 -> x0, blocking collectives: 50.2 us -> none  [body(): lax.all_gather(pos_label, 'label', axis=0, tiled=True)]
    all_to_all x0 -> x1, starting transfers between devices: none -> 13.2 us  [body(): lax.all_to_all(jnp.stack([pos_label] * lax.axis_size('label')), 'label',...]
    all_gather x1, blocking collectives: 41.3 us -> 47.2 us  [body(): lax.all_gather(shortlist, 'label', axis=0, tiled=True)]
    all_gather x1, blocking collectives: 44.9 us -> 41.1 us  [body(): cent_whole = lax.all_gather(cent_summed, 'label', axis=0, tiled=True)]
  transfers between devices with their start and end apart: 3 -> 4, of which waited for: 1 -> 1; matrix products, arithmetic and copies ran while one was open for 4% -> 5% of each run, Pallas kernels for 0% -> 0%
where the time goes in v1:
time: 342 us
  blocking collectives  183 us (54%)
  waiting for transfers between devices  101 us (30%)
  between operations  14 us (4%)
  matrix products  13.6 us (4%)
  starting transfers between devices  13.3 us (4%)
  local copies, waits for them, and re-layouts  11.3 us (3%)
  other arithmetic  5.54 us (2%)
    reduce_scatter x1, waiting for transfers between devices, body(): lax.psum_scatter((jnp.dot(grad, classifier, preferred_element_type=jnp.fl...  100 us
    psum x1, blocking collectives, body(): cent_summed = lax.psum(cent_acc, 'doc')  60.4 us
    all_gather x1, blocking collectives, body(): lax.all_gather(shortlist, 'label', axis=0, tiled=True)  47.2 us
    all_gather x1, blocking collectives, body(): cent_whole = lax.all_gather(cent_summed, 'label', axis=0, tiled=True)  41.1 us
    all_gather x1, blocking collectives, body(): all_cent = lax.all_gather(centroids, 'doc', axis=0, tiled=True)  34.5 us
    all_to_all x1, starting transfers between devices, body(): lax.all_to_all(jnp.stack([pos_label] * lax.axis_size('label')), 'label',...  13.2 us
  transfers between devices with their start and end apart: 4, of which 1 were waited for; matrix products, arithmetic and copies ran while one was open for 5% of the time, Pallas kernels for 0%

profile of v1, /device:TPU:8, one launch (start us, length us, event | category | flops | bytes accessed | tf_op | source)
XLA Modules:
  0.0 342.1 jit_solution(1461167035357559620)
XLA Ops:
  7.2 0.7 all-gather.2.cloned.1.call-update
  7.9 0.7 bitcast_or_fusion
  8.6 0.1 copy.49
  8.7 0.1 reshape.61
  8.8 1.3 gather_fusion
  10.1 0.1 reshape.64
  10.4 0.7 reshape.72
  11.1 13.2 %all-to-all-start = ((s32[32,1,128]{2,1,0:T(1,128)}), s32[32,1,128]{2,1,0:T(1,128)S(1)}, u32[]{:S(2)}, u32[]{:S(2)}) async-start(s32[32,1,128]{2,1,0:T(1,128)} %reshape.72), calls=%async_computation | async-start | bytes 32768 | tf_op jit(solution)/shard_map/all_to_all | solution.py:46
  24.3 47.2 %all_gather.12 = s32[1024,32]{1,0:T(8,128)S(1)} all-gather(s32[32,32]{1,0:T(8,128)S(1)} %copy-done.1), channel_id=1, replica_groups=mesh['doc'=16,'label'=32] {'label'}, dimensions={0}, use_global_device_ids=true | all-gather | bytes 135168 | tf_op jit(solution)/shard_map/all_gather | solution.py:44
  71.5 0.2 copy.47
  71.6 0.2 compare_reduce_fusion.1
  71.9 0.3 copy.48
  72.2 0.5 broadcast.117
  72.7 0.7 reduce
  73.4 0.1 reshape.73
  73.5 0.1 eq.46
  73.6 3.8 %compare_reduce_fusion = pred[1024,1024]{1,0:T(8,128)(4,1)} fusion(s32[1024]{0:T(1024)S(1)} %iota_add_fusion, s32[1024,4]{0,1:T(4,128)S(1)} %eq.46), kind=kLoop, calls=%fused_computation.1 | loop fusion | flops 7340032 | bytes 1069056 | tf_op jit(solution)/shard_map/reduce_or | solution.py:17
  77.4 3.2 broadcast_in_dim.6
  80.6 4.5 %select_convert_fusion = bf16[1024,1024]{1,0:T(8,128)(2,1)S(1)} fusion(pred[1024,1024]{1,0:T(8,128)(4,1)} %compare_reduce_fusion, pred[128,8,8,128]{3,2,1,0:T(8,128)(4,1)S(1)} %bitcast.30, bf16[1024,768]{1,0:T(8,128)(2,1)} %all-gather.2.cloned.1.call-done, bf16[1024,768]{1,0:T(8,128)(2,1)S(1)} %copy-done), kind=kOutput, calls=%fused_computation.2 | convolution fusion | flops 1619001344 | bytes 7340032 | tf_op jit(solution)/shard_map/nd,ld->nl/dot_general | solution.py:14
  85.1 1.3 copy-done.5
  86.5 3.0 convolution_convert_fusion
  89.6 34.5 %all_gather.14 = bf16[256,768]{1,0:T(8,128)(2,1)S(1)} all-gather(bf16[16,768]{1,0:T(8,128)(2,1)S(1)} %copy-done.3), channel_id=1, replica_groups=mesh['doc'=16,'label'=32] {'doc'}, dimensions={0}, use_global_device_ids=true | all-gather | bytes 417792 | tf_op jit(solution)/shard_map/all_gather | solution.py:40
  124.1 0.1 compare_reduce_fusion.2
  124.2 0.5 fusion.6
  124.7 3.4 fusion.16
  128.1 1.8 add_convert_fusion
  130.0 0.3 fusion.15
  130.3 60.4 %psum.15 = f32[8,768]{1,0:T(8,128)S(1)} all-reduce(f32[8,768]{1,0:T(8,128)S(1)} %fusion.15), channel_id=1, replica_groups=mesh['doc'=16,'label'=32] {'doc'}, use_global_device_ids=true, to_apply=%region_4.5 | all-reduce | flops 6144 | bytes 49152 | tf_op jit(solution)/shard_map/psum | solution.py:62
  190.7 41.1 %all_gather.15 = f32[256,768]{1,0:T(8,128)S(1)} all-gather(f32[8,768]{1,0:T(8,128)S(1)} %psum.15), channel_id=1, replica_groups=mesh['doc'=16,'label'=32] {'label'}, dimensions={0}, use_global_device_ids=true | all-gather | bytes 811008 | tf_op jit(solution)/shard_map/all_gather | solution.py:63
  231.8 0.6 constant_dynamic-slice_fusion
  232.5 100.5 %reduce-scatter.2.cloned.1.call-done = bf16[32,768]{1,0:T(8,128)(2,1)} async-done(((bf16[1024,768]{1,0:T(8,128)(2,1)}), bf16[32,768]{1,0:T(8,128)(2,1)}) %reduce-scatter.2.cloned.1.call-update) | async-done | bytes 49168 | tf_op jit(solution)/shard_map/reduce_scatter | solution.py:52
  333.0 2.7 copy.55
  (26 shorter events, 0.3 us)
Async XLA Ops:
  7.2 73.4 %copy-start = (bf16[1024,768]{1,0:T(8,128)(2,1)S(1)}, bf16[1024,768]{1,0:T(8,128)(2,1)}, u32[]{:S(2)}) copy-start(bf16[1024,768]{1,0:T(8,128)(2,1)} %param.6) | copy-start | bytes 4718596
  7.2 1.6 copy-start.1
  7.2 70.2 %all-gather.2.cloned.1.call-start = ((), (), s32[]{:S(2)}) async-start(), calls=%async_computation.2 | async-start | bytes 1622016 | tf_op jit(solution)/shard_map/all_gather | solution.py:43
  8.8 1.5 copy-start.4
  11.1 61.1 %all-to-all-start = ((s32[32,1,128]{2,1,0:T(1,128)}), s32[32,1,128]{2,1,0:T(1,128)S(1)}, u32[]{:S(2)}, u32[]{:S(2)}) async-start(s32[32,1,128]{2,1,0:T(1,128)} %reshape.72), calls=%async_computation | async-start | bytes 32768 | tf_op jit(solution)/shard_map/all_to_all | solution.py:46
  24.2 208.2 %all-reduce.2.cloned.1.call-start = ((), (), s32[]{:S(2)}) async-start(), calls=%async_computation.3 | async-start | bytes 3145728 | tf_op jit(solution)/shard_map/psum | solution.py:61
  80.6 5.9 %copy-start.2 = (bf16[1024,768]{1,0:T(8,128)(2,1)S(1)}, bf16[1024,768]{1,0:T(8,128)(2,1)}, u32[]{:S(2)}) copy-start(bf16[1024,768]{1,0:T(8,128)(2,1)} %all-gather.2.cloned.1.call-done) | copy-start | bytes 4718596
  85.1 1.4 copy-start.5
  86.5 3.1 copy-start.3
  89.6 243.4 %reduce-scatter.2.cloned.1.call-start = ((), (), s32[]{:S(2)}) async-start(), calls=%async_computation.4 | async-start | bytes 1622016 | tf_op jit(solution)/shard_map/reduce_scatter | solution.py:52
Sparse Core Ops, SparseCore 0:
  11.1 63.6 all-gather.1
  89.7 140.2 all-reduce.1
  235.0 97.9 reduce-scatter.1
